TPU v7x, 32 devices: a whole 2x2x4 slice. The times are simulated.
32 devices in a mesh: dp: 8 (over z, y), seq: 4 (over x, core).
Axes of the slice: x: 2, y: 2, z: 4, core: 2. Of those that a mesh axis runs over, the one named last changes fastest.
Arguments:
- frames: bfloat16 [8, 512, 1536], P('dp', 'seq'), may hold values from -6 to 6
- lengths: int32 [8, 4], P('dp'), may hold values from 1 to 256, 512 in all within a row
- ln1_gain: float32 [1536], replicated, may hold values from 0.5 to 12
- ln2_gain: float32 [1536], replicated, may hold values from 0.5 to 1.5
- w_qkv: bfloat16 [1536, 3, 1536], P('dp', None, 'seq'), may hold values from -0.15625 to 0.15625
- w_out: bfloat16 [1536, 1536], P('seq', 'dp'), may hold values from -0.15625 to 0.15625
- w_glu: bfloat16 [1536, 2, 1536], P('dp', None, 'seq'), may hold values from -0.15625 to 0.15625
- dw_kernel: bfloat16 [31, 1536], P(None, 'seq'), may hold values from -1 to 1
- w_proj: bfloat16 [1536, 1536], P('seq', 'dp'), may hold values from -0.15625 to 0.15625
Outputs:
- block_out: bfloat16 [8, 512, 1536], P('dp', 'seq')
Inputs may be any that keep to these rules, and one draw needn't show every extreme that they name: `lengths`: each row sums to 512, and its largest entry is 256.
All inputs are finite; a program needn't handle non-finite values.
Results may differ from a plain program's by a relative error of at most 0.013.
The roundings to bfloat16 on the way count: a program that leaves them out, or rounds other values in their place, can miss the bound.
Values may be sent and summed in bfloat16 or wider, within the bound.
No kernel may reach another device: no remote copies, remote signals or barrier semaphores. Data moves between devices by JAX's collectives and lax.ppermute only.
A program may use at most 64 MiB of HBM per device.

v0:
```python
import jax
import jax.numpy as jnp
from jax import lax
from jax.sharding import PartitionSpec as P

HD = 96


def layer_norm(values, gain_vec):
    mean_value = jnp.mean(values, axis=-1, keepdims=True)
    centered = values - mean_value
    variance = jnp.mean(centered * centered, axis=-1, keepdims=True)
    return (centered * lax.rsqrt(variance + 1e-05) * gain_vec).astype(jnp.bfloat16)


def segment_of(record_ends, positions):
    return jnp.sum((positions[:, None] >= record_ends[None, :]).astype(jnp.int32), axis=1)


def seq_gather(block):
    count = lax.axis_size("seq")
    me = lax.axis_index("seq")
    parts = [block]
    for shift in range(1, count):
        parts.append(lax.ppermute(block, "seq", [(i, (i - shift) % count) for i in range(count)]))
    ring = jnp.concatenate(parts + parts, axis=0)
    rows = block.shape[0]
    return lax.dynamic_slice_in_dim(ring, (count - me) % count * rows, count * rows, axis=0)


def seq_scatter_sum(full):
    count = lax.axis_size("seq")
    me = lax.axis_index("seq")
    rows = full.shape[0] // count
    total = lax.dynamic_slice_in_dim(full, me * rows, rows, axis=0).astype(jnp.float32)
    for shift in range(1, count):
        piece = lax.dynamic_slice_in_dim(full, (me + shift) % count * rows, rows, axis=0)
        got = lax.ppermute(piece, "seq", [(i, (i + shift) % count) for i in range(count)])
        total = total + got.astype(jnp.float32)
    return total


def attend(projected, seg_all, head_size):
    group_rows = projected.shape[0]
    block_rows = 512
    heads_here = projected.shape[2] // head_size
    split = projected.reshape(group_rows, 3, heads_here, head_size)
    queries = split[:, 0]
    keys = split[:, 1]
    values = split[:, 2]
    blocks = group_rows // block_rows
    scale = 1.0 / head_size**0.5

    def one_block(block_data):
        query_block, seg_block = block_data
        scores = (
            jnp.einsum("qhe,khe->hqk", query_block, keys, preferred_element_type=jnp.float32)
            * scale
        )
        allowed = seg_block[:, None] == seg_all[None, :]
        scores = jnp.where(allowed[None], scores, -1e30)
        top_score = jnp.max(scores, axis=-1, keepdims=True)
        weights = jnp.exp(scores - top_score)
        probs = (weights / jnp.sum(weights, axis=-1, keepdims=True)).astype(jnp.bfloat16)
        mixed = jnp.einsum("hqk,khe->qhe", probs, values, preferred_element_type=jnp.float32)
        return mixed.astype(jnp.bfloat16).reshape(block_rows, heads_here * head_size)

    result = lax.map(
        one_block,
        (
            queries.reshape(blocks, block_rows, heads_here, head_size),
            seg_all.reshape(blocks, block_rows),
        ),
    )
    return result.reshape(group_rows, heads_here * head_size)


def depthwise(padded, kernel, seg_here, seg_near, count):
    total_acc = jnp.zeros((count, padded.shape[1]), jnp.float32)
    for tap_index in range(kernel.shape[0]):
        window = padded[tap_index : tap_index + count].astype(jnp.float32)
        same = (seg_near[tap_index : tap_index + count] == seg_here)[:, None]
        total_acc = total_acc + jnp.where(same, window * kernel[tap_index].astype(jnp.float32), 0.0)
    return jax.nn.silu(total_acc).astype(jnp.bfloat16)


def on_device(frames, lengths, ln1_gain, ln2_gain, w_qkv, w_out, w_glu, dw_kernel, w_proj):
    frame_rows = frames.shape[1]
    model_width = frames.shape[2]
    seq_count = lax.axis_size("seq")
    group_rows = frame_rows * seq_count
    group_width = model_width // seq_count
    kernel_reach = dw_kernel.shape[0] // 2
    qkv_matrix = lax.all_gather(
        w_qkv.reshape(w_qkv.shape[0], 3 * group_width), "dp", axis=0, tiled=True
    )
    out_local = lax.all_gather(w_out, "dp", axis=1, tiled=True)
    glu_matrix = lax.all_gather(
        w_glu.reshape(w_glu.shape[0], 2 * group_width), "dp", axis=0, tiled=True
    )
    proj_local = lax.all_gather(w_proj, "dp", axis=1, tiled=True)
    inputs = frames[0].astype(jnp.float32)
    record_ends = jnp.cumsum(lengths[0])
    seg_all = segment_of(record_ends, jnp.arange(group_rows, dtype=jnp.int32))
    normed1 = layer_norm(inputs, ln1_gain)
    projected = (
        jnp.dot(seq_gather(normed1), qkv_matrix, preferred_element_type=jnp.float32)
        .astype(jnp.bfloat16)
        .reshape(group_rows, 3, group_width)
    )
    attended = attend(projected, seg_all, HD)
    attn_sum = seq_scatter_sum(
        jnp.dot(attended, out_local, preferred_element_type=jnp.float32).astype(jnp.bfloat16)
    )
    middle = (inputs + attn_sum).astype(jnp.bfloat16)
    normed2 = layer_norm(middle.astype(jnp.float32), ln2_gain)
    shard_piece = seq_gather(normed2)
    paired = jnp.dot(shard_piece, glu_matrix, preferred_element_type=jnp.float32).reshape(
        shard_piece.shape[0], 2, group_width
    )
    gated = (paired[:, 0] * jax.nn.sigmoid(paired[:, 1])).astype(jnp.bfloat16)
    padded = jnp.pad(gated, ((kernel_reach, kernel_reach), (0, 0)))
    near_positions = jnp.arange(-kernel_reach, group_rows + kernel_reach, dtype=jnp.int32)
    activated = depthwise(
        padded, dw_kernel, seg_all, segment_of(record_ends, near_positions), group_rows
    )
    conv_out = seq_scatter_sum(
        jnp.dot(activated, proj_local, preferred_element_type=jnp.float32).astype(jnp.bfloat16)
    )
    results = [(middle.astype(jnp.float32) + conv_out).astype(jnp.bfloat16)]
    return jnp.stack(results, axis=0)


def solution(mesh):
    in_specs = (
        P("dp", "seq", None),
        P("dp", None),
        P(),
        P(),
        P("dp", None, "seq"),
        P("seq", "dp"),
        P("dp", None, "seq"),
        P(None, "seq"),
        P("seq", "dp"),
    )
    out_specs = P("dp", "seq", None)
    return jax.shard_map(
        on_device, mesh=mesh, in_specs=in_specs, out_specs=out_specs, check_vma=False
    )
```

profile of v0, /device:TPU:1, one launch (start us, length us, event | category | flops | bytes accessed | tf_op | source)
XLA Modules:
  0.0 247.0 jit_solution(16871168828461402253)
XLA Ops:
  6.5 1.9 copy.27
  14.4 2.7 %collective-permute-start.1 = (bf16[128,1536]{1,0:T(8,128)(2,1)S(1)}, bf16[128,1536]{1,0:T(8,128)(2,1)S(1)}, u32[]{:S(2)}, u32[]{:S(2)}) collective-permute-start(bf16[128,1536]{1,0:T(8,128)(2,1)S(1)} %get-tuple-element.62), channel_id=1, source_target_pairs={{0,2},{1,3},{2,0},{3,1},{4,6},{5,7},{6,4},{7,5},{8,10},{9,11},{10,... | collective-permute-start | bytes 1179656 | tf_op jit(solution)/shard_map/ppermute | solution.py:25
  19.0 8.0 %collective-permute-done = bf16[128,1536]{1,0:T(8,128)(2,1)S(1)} collective-permute-done((bf16[128,1536]{1,0:T(8,128)(2,1)S(1)}, bf16[128,1536]{1,0:T(8,128)(2,1)S(1)}, u32[]{:S(2)}, u32[]{:S(2)}) %collective-permute-start) | collective-permute-done | bytes 393248 | tf_op jit(solution)/shard_map/ppermute | solution.py:25
  28.6 5.9 %collective-permute-done.2 = bf16[128,1536]{1,0:T(8,128)(2,1)S(1)} collective-permute-done((bf16[128,1536]{1,0:T(8,128)(2,1)S(1)}, bf16[128,1536]{1,0:T(8,128)(2,1)S(1)}, u32[]{:S(2)}, u32[]{:S(2)}) %collective-permute-start.2) | collective-permute-done | bytes 393248 | tf_op jit(solution)/shard_map/ppermute | solution.py:25
  38.4 37.5 %all-gather.5.cloned.1.call-done = bf16[1536,1152]{1,0:T(8,128)(2,1)} async-done(((bf16[192,1152]{1,0:T(8,128)(2,1)}), bf16[1536,1152]{1,0:T(8,128)(2,1)}) %all-gather.5.cloned.1.call-update) | async-done | bytes 3538960 | tf_op jit(solution)/shard_map/all_gather | solution.py:94
  75.9 4.7 %convolution_convert_fusion = bf16[512,1152]{1,0:T(8,128)(2,1)S(1)} fusion(bf16[1536,1152]{1,0:T(8,128)(2,1)} %all-gather.5.cloned.1.call-done, bf16[1024,1536]{1,0:T(8,128)(2,1)} %constant_dynamic-update-slice_fusion, s32[]{:T(128)S(6)} %select_n.147), kind=kOutput, calls=%fused_computation.5 | convolution fusion | flops 1812529152 | bytes 6291460 | tf_op jit(solution)/shard_map/dot_general | solution.py:107
  81.2 3.6 %fusion.45 = (f32[4,512]{1,0:T(4,128)S(1)}, f32[4,512,512]{1,2,0:T(8,128)}) fusion(pred[512,512]{0,1:T(8,128)(4,1)S(1)} %broadcast_compare_fusion, bf16[512,3,4,96]{0,3,2,1:T(8,128)(2,1)S(1)} %bitcast.65), kind=kOutput, calls=%fused_computation.155 | convolution fusion | flops 205521408 | bytes 5251072 | tf_op jit(solution)/shard_map/while/body/eval_jaxpr/sub | solution.py:63
  84.8 2.8 %fusion.9 = bf16[4,96,512]{2,1,0:T(8,128)(2,1)S(1)} fusion(f32[4,512,512]{1,2,0:T(8,128)} %get-tuple-element.103, f32[4,512]{1,0:T(4,128)S(1)} %get-tuple-element.102, bf16[512,3,4,96]{0,3,2,1:T(8,128)(2,1)S(1)} %bitcast.66), kind=kOutput, calls=%fused_computation.15 | convolution fusion | flops 203620352 | bytes 4988928 | tf_op jit(solution)/shard_map/while/body/eval_jaxpr/hqk,khe->qhe/dot_general | solution.py:65
  87.6 29.8 %all-gather.7.cloned.1.call-done = bf16[384,1536]{0,1:T(8,128)(2,1)} async-done(((bf16[384,192]{0,1:T(8,128)(2,1)}), bf16[384,1536]{0,1:T(8,128)(2,1)}) %all-gather.7.cloned.1.call-update) | async-done | bytes 1179664 | tf_op jit(solution)/shard_map/all_gather | solution.py:97
  117.4 2.3 convolution_convert_fusion.2
  119.8 3.1 %collective-permute-start.3 = (bf16[128,1536]{1,0:T(8,128)(2,1)S(1)}, bf16[128,1536]{1,0:T(8,128)(2,1)S(1)}, u32[]{:S(2)}, u32[]{:S(2)}) collective-permute-start(bf16[128,1536]{1,0:T(8,128)(2,1)S(1)} %get-tuple-element.68), channel_id=1, source_target_pairs={{0,1},{1,2},{2,3},{3,0},{4,5},{5,6},{6,7},{7,4},{8,9},{9,10},{10,1... | collective-permute-start | bytes 1179656 | tf_op jit(solution)/shard_map/ppermute | solution.py:38
  124.7 6.4 %collective-permute-done.3 = bf16[128,1536]{1,0:T(8,128)(2,1)S(1)} collective-permute-done((bf16[128,1536]{1,0:T(8,128)(2,1)S(1)}, bf16[128,1536]{1,0:T(8,128)(2,1)S(1)}, u32[]{:S(2)}, u32[]{:S(2)}) %collective-permute-start.3) | collective-permute-done | bytes 393248 | tf_op jit(solution)/shard_map/ppermute | solution.py:38
  131.2 9.5 %collective-permute-done.4 = bf16[128,1536]{1,0:T(8,128)(2,1)} collective-permute-done((bf16[128,1536]{1,0:T(8,128)(2,1)S(1)}, bf16[128,1536]{1,0:T(8,128)(2,1)}, u32[]{:S(2)}, u32[]{:S(2)}) %collective-permute-start.4) | collective-permute-done | bytes 393248 | tf_op jit(solution)/shard_map/ppermute | solution.py:38
  145.5 2.2 collective-permute-start.8
  147.8 8.0 %collective-permute-done.6 = bf16[128,1536]{1,0:T(8,128)(2,1)S(1)} collective-permute-done((bf16[128,1536]{1,0:T(8,128)(2,1)S(1)}, bf16[128,1536]{1,0:T(8,128)(2,1)S(1)}, u32[]{:S(2)}, u32[]{:S(2)}) %collective-permute-start.6) | collective-permute-done | bytes 393248 | tf_op jit(solution)/shard_map/ppermute | solution.py:25
  157.3 5.1 %collective-permute-done.8 = bf16[128,1536]{1,0:T(8,128)(2,1)S(1)} collective-permute-done((bf16[128,1536]{1,0:T(8,128)(2,1)S(1)}, bf16[128,1536]{1,0:T(8,128)(2,1)S(1)}, u32[]{:S(2)}, u32[]{:S(2)}) %collective-permute-start.8) | collective-permute-done | bytes 393248 | tf_op jit(solution)/shard_map/ppermute | solution.py:25
  166.3 4.2 %all-gather.9.cloned.1.call-done = bf16[1536,768]{1,0:T(8,128)(2,1)} async-done(((bf16[192,768]{1,0:T(8,128)(2,1)}), bf16[1536,768]{1,0:T(8,128)(2,1)}) %all-gather.9.cloned.1.call-update) | async-done | bytes 2359312 | tf_op jit(solution)/shard_map/all_gather | solution.py:98
  170.5 4.7 %fusion.6 = f32[512,768]{1,0:T(8,128)} fusion(bf16[1536,768]{1,0:T(8,128)(2,1)} %all-gather.9.cloned.1.call-done, bf16[1024,1536]{1,0:T(8,128)(2,1)} %constant_dynamic-update-slice_fusion.8, s32[]{:T(128)S(6)} %select_n.147), kind=kOutput, calls=%fused_computation.12 | convolution fusion | flops 1207959552 | bytes 5505028 | tf_op jit(solution)/shard_map/dot_general | solution.py:118
  175.1 2.1 reshape.147
  178.9 33.2 %all-gather.11.cloned.1.call-done = bf16[384,1536]{0,1:T(8,128)(2,1)} async-done(((bf16[384,192]{0,1:T(8,128)(2,1)}), bf16[384,1536]{0,1:T(8,128)(2,1)}) %all-gather.11.cloned.1.call-update) | async-done | bytes 1179664 | tf_op jit(solution)/shard_map/all_gather | solution.py:101
  212.2 7.8 %convolution_convert_fusion.1 = bf16[512,1536]{1,0:T(8,128)(2,1)S(1)} fusion(bf16[384,1536]{0,1:T(8,128)(2,1)} %all-gather.11.cloned.1.call-done, bf16[512,384]{1,0:T(8,128)(2,1)S(1)} %fusion.32, f32[384]{0:T(512)S(1)} %get-tuple-element.55, f32[384]{0:T(512)S(1)} %get-tuple-element.56, f32[384]{0:T(512)S(1)} %get-tuple-element.18, ...), kind=kOutput, calls=%fused_computation.6 | convolution fusion | flops 629932032 | bytes 3209216 | tf_op jit(solution)/shard_map/dot_general | solution.py:128
  221.4 2.2 collective-permute-start.11
  223.8 5.1 %collective-permute-done.10 = bf16[128,1536]{1,0:T(8,128)(2,1)S(1)} collective-permute-done((bf16[128,1536]{1,0:T(8,128)(2,1)S(1)}, bf16[128,1536]{1,0:T(8,128)(2,1)S(1)}, u32[]{:S(2)}, u32[]{:S(2)}) %collective-permute-start.10) | collective-permute-done | bytes 393248 | tf_op jit(solution)/shard_map/ppermute | solution.py:38
  228.9 10.6 %collective-permute-done.11 = bf16[128,1536]{1,0:T(8,128)(2,1)S(1)} collective-permute-done((bf16[128,1536]{1,0:T(8,128)(2,1)S(1)}, bf16[128,1536]{1,0:T(8,128)(2,1)S(1)}, u32[]{:S(2)}, u32[]{:S(2)}) %collective-permute-start.11) | collective-permute-done | bytes 393248 | tf_op jit(solution)/shard_map/ppermute | solution.py:38
  (108 shorter events, 30.2 us)
Async XLA Ops:
  6.5 69.3 %all-gather.5.cloned.1.call-start = ((), (), s32[]{:S(2)}) async-start(), calls=%async_computation | async-start | bytes 3981312 | tf_op jit(solution)/shard_map/all_gather | solution.py:94
  8.4 108.9 %all-gather.7.cloned.1.call-start = ((), (), s32[]{:S(2)}) async-start(), calls=%async_computation.1 | async-start | bytes 1327104 | tf_op jit(solution)/shard_map/all_gather | solution.py:97
  9.2 161.3 %all-gather.9.cloned.1.call-start = ((), (), s32[]{:S(2)}) async-start(), calls=%async_computation.2 | async-start | bytes 2654208 | tf_op jit(solution)/shard_map/all_gather | solution.py:98
  11.0 201.1 %all-gather.11.cloned.1.call-start = ((), (), s32[]{:S(2)}) async-start(), calls=%async_computation.3 | async-start | bytes 1327104 | tf_op jit(solution)/shard_map/all_gather | solution.py:101
  14.4 12.7 %collective-permute-start = (bf16[128,1536]{1,0:T(8,128)(2,1)S(1)}, bf16[128,1536]{1,0:T(8,128)(2,1)S(1)}, u32[]{:S(2)}, u32[]{:S(2)}) collective-permute-start(bf16[128,1536]{1,0:T(8,128)(2,1)S(1)} %get-tuple-element.62), channel_id=1, source_target_pairs={{0,3},{1,0},{2,1},{3,2},{4,7},{5,4},{6,5},{7,6},{8,11},{9,8},{10,9... | collective-permute-start | bytes 1179656 | tf_op jit(solution)/shard_map/ppermute | solution.py:25
  14.4 13.4 %collective-permute-start.1 = (bf16[128,1536]{1,0:T(8,128)(2,1)S(1)}, bf16[128,1536]{1,0:T(8,128)(2,1)S(1)}, u32[]{:S(2)}, u32[]{:S(2)}) collective-permute-start(bf16[128,1536]{1,0:T(8,128)(2,1)S(1)} %get-tuple-element.62), channel_id=1, source_target_pairs={{0,2},{1,3},{2,0},{3,1},{4,6},{5,7},{6,4},{7,5},{8,10},{9,11},{10,... | collective-permute-start | bytes 1179656 | tf_op jit(solution)/shard_map/ppermute | solution.py:25
  17.1 17.4 %collective-permute-start.2 = (bf16[128,1536]{1,0:T(8,128)(2,1)S(1)}, bf16[128,1536]{1,0:T(8,128)(2,1)S(1)}, u32[]{:S(2)}, u32[]{:S(2)}) collective-permute-start(bf16[128,1536]{1,0:T(8,128)(2,1)S(1)} %get-tuple-element.62), channel_id=1, source_target_pairs={{0,1},{1,2},{2,3},{3,0},{4,5},{5,6},{6,7},{7,4},{8,9},{9,10},{10,1... | collective-permute-start | bytes 1179656 | tf_op jit(solution)/shard_map/ppermute | solution.py:25
  119.8 11.4 %collective-permute-start.3 = (bf16[128,1536]{1,0:T(8,128)(2,1)S(1)}, bf16[128,1536]{1,0:T(8,128)(2,1)S(1)}, u32[]{:S(2)}, u32[]{:S(2)}) collective-permute-start(bf16[128,1536]{1,0:T(8,128)(2,1)S(1)} %get-tuple-element.68), channel_id=1, source_target_pairs={{0,1},{1,2},{2,3},{3,0},{4,5},{5,6},{6,7},{7,4},{8,9},{9,10},{10,1... | collective-permute-start | bytes 1179656 | tf_op jit(solution)/shard_map/ppermute | solution.py:38
  122.8 17.9 %collective-permute-start.4 = (bf16[128,1536]{1,0:T(8,128)(2,1)S(1)}, bf16[128,1536]{1,0:T(8,128)(2,1)}, u32[]{:S(2)}, u32[]{:S(2)}) collective-permute-start(bf16[128,1536]{1,0:T(8,128)(2,1)S(1)} %get-tuple-element.70), channel_id=1, source_target_pairs={{0,2},{1,3},{2,0},{3,1},{4,6},{5,7},{6,4},{7,5},{8,10},{9,11},{10,... | collective-permute-start | bytes 1179656 | tf_op jit(solution)/shard_map/ppermute | solution.py:38
  123.1 18.2 %collective-permute-start.5 = (bf16[128,1536]{1,0:T(8,128)(2,1)S(1)}, bf16[128,1536]{1,0:T(8,128)(2,1)}, u32[]{:S(2)}, u32[]{:S(2)}) collective-permute-start(bf16[128,1536]{1,0:T(8,128)(2,1)S(1)} %get-tuple-element.69), channel_id=1, source_target_pairs={{0,3},{1,0},{2,1},{3,2},{4,7},{5,4},{6,5},{7,6},{8,11},{9,8},{10,9... | collective-permute-start | bytes 1179656 | tf_op jit(solution)/shard_map/ppermute | solution.py:38
  144.0 11.7 %collective-permute-start.6 = (bf16[128,1536]{1,0:T(8,128)(2,1)S(1)}, bf16[128,1536]{1,0:T(8,128)(2,1)S(1)}, u32[]{:S(2)}, u32[]{:S(2)}) collective-permute-start(bf16[128,1536]{1,0:T(8,128)(2,1)S(1)} %get-tuple-element.58), channel_id=1, source_target_pairs={{0,3},{1,0},{2,1},{3,2},{4,7},{5,4},{6,5},{7,6},{8,11},{9,8},{10,9... | collective-permute-start | bytes 1179656 | tf_op jit(solution)/shard_map/ppermute | solution.py:25
  144.1 12.4 %collective-permute-start.7 = (bf16[128,1536]{1,0:T(8,128)(2,1)S(1)}, bf16[128,1536]{1,0:T(8,128)(2,1)S(1)}, u32[]{:S(2)}, u32[]{:S(2)}) collective-permute-start(bf16[128,1536]{1,0:T(8,128)(2,1)S(1)} %get-tuple-element.58), channel_id=1, source_target_pairs={{0,2},{1,3},{2,0},{3,1},{4,6},{5,7},{6,4},{7,5},{8,10},{9,11},{10,... | collective-permute-start | bytes 1179656 | tf_op jit(solution)/shard_map/ppermute | solution.py:25
  145.5 16.9 %collective-permute-start.8 = (bf16[128,1536]{1,0:T(8,128)(2,1)S(1)}, bf16[128,1536]{1,0:T(8,128)(2,1)S(1)}, u32[]{:S(2)}, u32[]{:S(2)}) collective-permute-start(bf16[128,1536]{1,0:T(8,128)(2,1)S(1)} %get-tuple-element.58), channel_id=1, source_target_pairs={{0,1},{1,2},{2,3},{3,0},{4,5},{5,6},{6,7},{7,4},{8,9},{9,10},{10,1... | collective-permute-start | bytes 1179656 | tf_op jit(solution)/shard_map/ppermute | solution.py:25
  177.3 34.8 %copy-start.5 = (pred[512]{0:T(512)(128)(4,1)S(1)}, pred[512]{0:T(512)(128)(4,1)}, u32[]{:S(2)}) copy-start(pred[512]{0:T(512)(128)(4,1)} %get-tuple-element.71) | copy-start | bytes 1540
  177.3 34.8 %copy-start.6 = (pred[512]{0:T(512)(128)(4,1)S(1)}, pred[512]{0:T(512)(128)(4,1)}, u32[]{:S(2)}) copy-start(pred[512]{0:T(512)(128)(4,1)} %get-tuple-element.72) | copy-start | bytes 1540
  177.3 34.8 %copy-start.7 = (pred[512]{0:T(512)(128)(4,1)S(1)}, pred[512]{0:T(512)(128)(4,1)}, u32[]{:S(2)}) copy-start(pred[512]{0:T(512)(128)(4,1)} %get-tuple-element.73) | copy-start | bytes 1540
  177.3 34.8 %copy-start.8 = (pred[512]{0:T(512)(128)(4,1)S(1)}, pred[512]{0:T(512)(128)(4,1)}, u32[]{:S(2)}) copy-start(pred[512]{0:T(512)(128)(4,1)} %get-tuple-element.74) | copy-start | bytes 1540
  177.3 34.8 %copy-start.9 = (pred[512]{0:T(512)(128)(4,1)S(1)}, pred[512]{0:T(512)(128)(4,1)}, u32[]{:S(2)}) copy-start(pred[512]{0:T(512)(128)(4,1)} %get-tuple-element.75) | copy-start | bytes 1540
  177.3 34.8 %copy-start.10 = (pred[512]{0:T(512)(128)(4,1)S(1)}, pred[512]{0:T(512)(128)(4,1)}, u32[]{:S(2)}) copy-start(pred[512]{0:T(512)(128)(4,1)} %get-tuple-element.76) | copy-start | bytes 1540
  177.3 34.8 %copy-start.11 = (pred[512]{0:T(512)(128)(4,1)S(1)}, pred[512]{0:T(512)(128)(4,1)}, u32[]{:S(2)}) copy-start(pred[512]{0:T(512)(128)(4,1)} %get-tuple-element.77) | copy-start | bytes 1540
  177.3 34.8 %copy-start.12 = (pred[512]{0:T(512)(128)(4,1)S(1)}, pred[512]{0:T(512)(128)(4,1)}, u32[]{:S(2)}) copy-start(pred[512]{0:T(512)(128)(4,1)} %get-tuple-element.78) | copy-start | bytes 1540
  220.2 8.7 %collective-permute-start.10 = (bf16[128,1536]{1,0:T(8,128)(2,1)S(1)}, bf16[128,1536]{1,0:T(8,128)(2,1)S(1)}, u32[]{:S(2)}, u32[]{:S(2)}) collective-permute-start(bf16[128,1536]{1,0:T(8,128)(2,1)S(1)} %get-tuple-element.65), channel_id=1, source_target_pairs={{0,2},{1,3},{2,0},{3,1},{4,6},{5,7},{6,4},{7,5},{8,10},{9,11},{10,... | collective-permute-start | bytes 1179656 | tf_op jit(solution)/shard_map/ppermute | solution.py:38
  221.4 18.1 %collective-permute-start.11 = (bf16[128,1536]{1,0:T(8,128)(2,1)S(1)}, bf16[128,1536]{1,0:T(8,128)(2,1)S(1)}, u32[]{:S(2)}, u32[]{:S(2)}) collective-permute-start(bf16[128,1536]{1,0:T(8,128)(2,1)S(1)} %get-tuple-element.64), channel_id=1, source_target_pairs={{0,3},{1,0},{2,1},{3,2},{4,7},{5,4},{6,5},{7,6},{8,11},{9,8},{10,9... | collective-permute-start | bytes 1179656 | tf_op jit(solution)/shard_map/ppermute | solution.py:38
  223.6 15.9 %collective-permute-start.9 = (bf16[128,1536]{1,0:T(8,128)(2,1)S(1)}, bf16[128,1536]{1,0:T(8,128)(2,1)S(1)}, u32[]{:S(2)}, u32[]{:S(2)}) collective-permute-start(bf16[128,1536]{1,0:T(8,128)(2,1)S(1)} %get-tuple-element.63), channel_id=1, source_target_pairs={{0,1},{1,2},{2,3},{3,0},{4,5},{5,6},{6,7},{7,4},{8,9},{9,10},{10,1... | collective-permute-start | bytes 1179656 | tf_op jit(solution)/shard_map/ppermute | solution.py:38
  (16 other events, 438.8 us)
Sparse Core Ops, SparseCore 0:
  9.5 66.2 all-gather.4
  78.1 39.2 all-gather.6
  119.5 50.8 all-gather.8
  172.5 39.5 all-gather.10
where the time goes:
time: 247 us
  waiting for transfers between devices  165 us (67%)
  matrix products  25.8 us (10%)
  local copies, waits for them, and re-layouts  18.8 us (8%)
  starting transfers between devices  14.8 us (6%)
  between operations  13.6 us (6%)
  other arithmetic  9.38 us (4%)
    all_gather x1, waiting for transfers between devices, on_device(): lax.all_gather(w_qkv.reshape(w_qkv.shape[0], 3 * group_width), 'dp', axis...  37.5 us
    all_gather x1, waiting for transfers between devices, on_device(): proj_local = lax.all_gather(w_proj, 'dp', axis=1, tiled=True)  33.2 us
    ppermute x6, waiting for transfers between devices, seq_scatter_sum(): lax.ppermute(piece, 'seq', [(i, (i + shift) % count) for i in range(count)])  32.3 us
    all_gather x1, waiting for transfers between devices, on_device(): out_local = lax.all_gather(w_out, 'dp', axis=1, tiled=True)  29.8 us
    ppermute x6, waiting for transfers between devices, seq_gather(): lax.ppermute(block, 'seq', [(i, (i - shift) % count) for i in range(count)])  26.9 us
    unnamed x61, local copies, waits for them, and re-layouts  11.2 us
    dot_general x1, matrix products, on_device(): jnp.dot(activated, proj_local, preferred_element_type=jnp.float32)  7.81 us
    ppermute x6, starting transfers between devices, seq_gather(): lax.ppermute(block, 'seq', [(i, (i - shift) % count) for i in range(count)])  7.57 us
  transfers between devices with their start and end apart: 16, of which 13 were waited for; matrix products, arithmetic and copies ran while one was open for 17% of the time, Pallas kernels for 0%

commit v1 on v0

--- a/solution.py
+++ b/solution.py
@@ -4,6 +4,17 @@
 from jax.sharding import PartitionSpec as P
 
 HD = 96
+
+
+def gather_by_hops(x, axis, dim):
+    devices = lax.axis_size(axis)
+    right = [(i, (i + 1) % devices) for i in range(devices)]
+    blocks = [x]
+    for far in range(1, devices):
+        blocks = [lax.ppermute(blocks[0], axis, right), *blocks]
+    out = jnp.concatenate(blocks, axis=dim)
+    shift = (lax.axis_index(axis) + 1) * blocks[-1].shape[dim]
+    return jnp.roll(out, shift, axis=dim)
 
 
 def layer_norm(values, gain_vec):
@@ -94,7 +105,7 @@
     qkv_matrix = lax.all_gather(
         w_qkv.reshape(w_qkv.shape[0], 3 * group_width), "dp", axis=0, tiled=True
     )
-    out_local = lax.all_gather(w_out, "dp", axis=1, tiled=True)
+    out_local = gather_by_hops(w_out, "dp", 1)
     glu_matrix = lax.all_gather(
         w_glu.reshape(w_glu.shape[0], 2 * group_width), "dp", axis=0, tiled=True
     )

time: 247 us -> 222 us (0.90)
  waiting for transfers between devices: 165 us -> 122 us
  local copies, waits for them, and re-layouts: 18.8 us -> 28.4 us
  starting transfers between devices: 14.8 us -> 22 us
    ppermute x0 -> x7, waiting for transfers between devices: none -> 55.3 us  [gather_by_hops(): blocks = [lax.ppermute(blocks[0], axis, right), *blocks]]
    all_gather x1, waiting for transfers between devices: 37.5 us -> 0.52 us  [on_device(): lax.all_gather(w_qkv.reshape(w_qkv.shape[0], 3 * group_width), 'dp', axis...]
    all_gather x1 -> x0, waiting for transfers between devices: 29.8 us -> none  [on_device(): out_local = lax.all_gather(w_out, 'dp', axis=1, tiled=True)]
    ppermute x6, waiting for transfers between devices: 26.9 us -> 10.2 us  [seq_gather(): lax.ppermute(block, 'seq', [(i, (i - shift) % count) for i in range(count)])]
    all_gather x1, waiting for transfers between devices: 33.2 us -> 21 us  [on_device(): proj_local = lax.all_gather(w_proj, 'dp', axis=1, tiled=True)]
    unnamed x61 -> x118, local copies, waits for them, and re-layouts: 11.2 us -> 21.4 us
    ppermute x6, starting transfers between devices: 7.15 us -> 12.8 us  [seq_scatter_sum(): lax.ppermute(piece, 'seq', [(i, (i + shift) % count) for i in range(count)])]
    all_gather x1, waiting for transfers between devices: 4.18 us -> 0.01 us  [on_device(): lax.all_gather(w_glu.reshape(w_glu.shape[0], 2 * group_width), 'dp', axis...]
  transfers between devices with their start and end apart: 16 -> 22, of which waited for: 13 -> 17; matrix products, arithmetic and copies ran while one was open for 17% -> 24% of each run, Pallas kernels for 0% -> 0%
where the time goes in v1:
time: 222 us
  waiting for transfers between devices  122 us (55%)
  local copies, waits for them, and re-layouts  28.4 us (13%)
  matrix products  25.1 us (11%)
  starting transfers between devices  22 us (10%)
  between operations  14 us (6%)
  other arithmetic  10.8 us (5%)
    ppermute x7, waiting for transfers between devices, gather_by_hops(): blocks = [lax.ppermute(blocks[0], axis, right), *blocks]  55.3 us
    ppermute x6, waiting for transfers between devices, seq_scatter_sum(): lax.ppermute(piece, 'seq', [(i, (i + shift) % count) for i in range(count)])  34.6 us
    unnamed x118, local copies, waits for them, and re-layouts  21.4 us
    all_gather x1, waiting for transfers between devices, on_device(): proj_local = lax.all_gather(w_proj, 'dp', axis=1, tiled=True)  21 us
    ppermute x6, starting transfers between devices, seq_scatter_sum(): lax.ppermute(piece, 'seq', [(i, (i + shift) % count) for i in range(count)])  12.8 us
    ppermute x6, waiting for transfers between devices, seq_gather(): lax.ppermute(block, 'seq', [(i, (i - shift) % count) for i in range(count)])  10.2 us
    dot_general x1, matrix products, on_device(): jnp.dot(activated, proj_local, preferred_element_type=jnp.float32)  8.08 us
    ppermute x6, starting transfers between devices, seq_gather(): lax.ppermute(block, 'seq', [(i, (i - shift) % count) for i in range(count)])  6.36 us
  transfers between devices with their start and end apart: 22, of which 17 were waited for; matrix products, arithmetic and copies ran while one was open for 24% of the time, Pallas kernels for 0%

profile of v1, /device:TPU:1, one launch (start us, length us, event | category | flops | bytes accessed | tf_op | source)
XLA Modules:
  0.0 221.9 jit_solution(12835087239390443769)
XLA Ops:
  11.8 2.7 %collective-permute-start.3 = (bf16[384,192]{0,1:T(8,128)(2,1)S(1)}, bf16[384,192]{0,1:T(8,128)(2,1)S(1)}, u32[]{:S(2)}, u32[]{:S(2)}) collective-permute-start(bf16[384,192]{0,1:T(8,128)(2,1)S(1)} %copy-done.1), channel_id=1, source_target_pairs={{0,4},{4,8},{8,12},{12,16},{16,20},{20,24},{24,28},{28,0},{1,5},{5... | collective-permute-start | bytes 442376 | tf_op jit(solution)/shard_map/ppermute | solution.py:14
  17.7 2.9 %collective-permute-done.3 = bf16[384,192]{0,1:T(8,128)(2,1)S(1)} collective-permute-done((bf16[384,192]{0,1:T(8,128)(2,1)S(1)}, bf16[384,192]{0,1:T(8,128)(2,1)S(1)}, u32[]{:S(2)}, u32[]{:S(2)}) %collective-permute-start.3) | collective-permute-done | bytes 147488 | tf_op jit(solution)/shard_map/ppermute | solution.py:14
  20.8 10.5 %collective-permute-done.4 = bf16[384,192]{0,1:T(8,128)(2,1)S(1)} collective-permute-done((bf16[384,192]{0,1:T(8,128)(2,1)S(1)}, bf16[384,192]{0,1:T(8,128)(2,1)S(1)}, u32[]{:S(2)}, u32[]{:S(2)}) %collective-permute-start.4) | collective-permute-done | bytes 147488 | tf_op jit(solution)/shard_map/ppermute | solution.py:14
  33.7 8.3 %collective-permute-done.5 = bf16[384,192]{0,1:T(8,128)(2,1)S(1)} collective-permute-done((bf16[384,192]{0,1:T(8,128)(2,1)S(1)}, bf16[384,192]{0,1:T(8,128)(2,1)S(1)}, u32[]{:S(2)}, u32[]{:S(2)}) %collective-permute-start.5) | collective-permute-done | bytes 147488 | tf_op jit(solution)/shard_map/ppermute | solution.py:14
  42.7 5.9 %collective-permute-done.6 = bf16[384,192]{0,1:T(8,128)(2,1)S(1)} collective-permute-done((bf16[384,192]{0,1:T(8,128)(2,1)S(1)}, bf16[384,192]{0,1:T(8,128)(2,1)S(1)}, u32[]{:S(2)}, u32[]{:S(2)}) %collective-permute-start.6) | collective-permute-done | bytes 147488 | tf_op jit(solution)/shard_map/ppermute | solution.py:14
  49.4 9.0 %collective-permute-done.7 = bf16[384,192]{0,1:T(8,128)(2,1)S(1)} collective-permute-done((bf16[384,192]{0,1:T(8,128)(2,1)S(1)}, bf16[384,192]{0,1:T(8,128)(2,1)S(1)}, u32[]{:S(2)}, u32[]{:S(2)}) %collective-permute-start.7) | collective-permute-done | bytes 147488 | tf_op jit(solution)/shard_map/ppermute | solution.py:14
  59.3 9.1 %collective-permute-done.8 = bf16[384,192]{0,1:T(8,128)(2,1)S(1)} collective-permute-done((bf16[384,192]{0,1:T(8,128)(2,1)S(1)}, bf16[384,192]{0,1:T(8,128)(2,1)S(1)}, u32[]{:S(2)}, u32[]{:S(2)}) %collective-permute-start.8) | collective-permute-done | bytes 147488 | tf_op jit(solution)/shard_map/ppermute | solution.py:14
  69.2 9.5 %collective-permute-done.9 = bf16[384,192]{0,1:T(8,128)(2,1)S(1)} collective-permute-done((bf16[384,192]{0,1:T(8,128)(2,1)S(1)}, bf16[384,192]{0,1:T(8,128)(2,1)S(1)}, u32[]{:S(2)}, u32[]{:S(2)}) %collective-permute-start.9) | collective-permute-done | bytes 147488 | tf_op jit(solution)/shard_map/ppermute | solution.py:14
  90.0 4.7 %convolution_convert_fusion = bf16[512,1152]{1,0:T(8,128)(2,1)S(1)} fusion(bf16[1536,1152]{1,0:T(8,128)(2,1)} %all-gather.4.cloned.1.call-done, bf16[1024,1536]{1,0:T(8,128)(2,1)} %constant_dynamic-update-slice_fusion, s32[]{:T(128)S(6)} %select_n.159), kind=kOutput, calls=%fused_computation.5 | convolution fusion | flops 1812529152 | bytes 6291460 | tf_op jit(solution)/shard_map/dot_general | solution.py:118
  95.3 3.6 %fusion.47 = (f32[4,512]{1,0:T(4,128)S(1)}, f32[4,512,512]{1,2,0:T(8,128)}) fusion(pred[512,512]{0,1:T(8,128)(4,1)S(1)} %broadcast_compare_fusion, bf16[512,3,4,96]{0,3,2,1:T(8,128)(2,1)S(1)} %bitcast.64), kind=kOutput, calls=%fused_computation.173 | convolution fusion | flops 205521408 | bytes 5251072 | tf_op jit(solution)/shard_map/while/body/eval_jaxpr/sub | solution.py:74
  99.0 2.8 %fusion.9 = bf16[4,96,512]{2,1,0:T(8,128)(2,1)S(1)} fusion(f32[4,512,512]{1,2,0:T(8,128)} %get-tuple-element.103, f32[4,512]{1,0:T(4,128)S(1)} %get-tuple-element.102, bf16[512,3,4,96]{0,3,2,1:T(8,128)(2,1)S(1)} %bitcast.65), kind=kOutput, calls=%fused_computation.15 | convolution fusion | flops 203620352 | bytes 4988928 | tf_op jit(solution)/shard_map/while/body/eval_jaxpr/hqk,khe->qhe/dot_general | solution.py:76
  101.8 2.3 %convolution_convert_fusion.2 = bf16[512,1536]{1,0:T(8,128)(2,1)S(1)} fusion(bf16[512,384]{0,1:T(8,128)(2,1)S(1)} %bitcast.72, bf16[384,3072]{0,1:T(8,128)(2,1)} %constant_dynamic-update-slice_fusion.8, s32[]{:T(128)S(6)} %select_n.162), kind=kOutput, calls=%fused_computation.7 | convolution fusion | flops 604766208 | bytes 3145732 | tf_op jit(solution)/shard_map/dot_general | solution.py:124
  104.2 8.8 %collective-permute-start.10 = (bf16[128,1536]{1,0:T(8,128)(2,1)S(1)}, bf16[128,1536]{1,0:T(8,128)(2,1)}, u32[]{:S(2)}, u32[]{:S(2)}) collective-permute-start(bf16[128,1536]{1,0:T(8,128)(2,1)S(1)} %get-tuple-element.68), channel_id=1, source_target_pairs={{0,1},{1,2},{2,3},{3,0},{4,5},{5,6},{6,7},{7,4},{8,9},{9,10},{10,1... | collective-permute-start | bytes 1179656 | tf_op jit(solution)/shard_map/ppermute | solution.py:49
  114.3 7.0 %collective-permute-done.10 = bf16[128,1536]{1,0:T(8,128)(2,1)} collective-permute-done((bf16[128,1536]{1,0:T(8,128)(2,1)S(1)}, bf16[128,1536]{1,0:T(8,128)(2,1)}, u32[]{:S(2)}, u32[]{:S(2)}) %collective-permute-start.10) | collective-permute-done | bytes 393248 | tf_op jit(solution)/shard_map/ppermute | solution.py:49
  121.4 9.4 %collective-permute-done.11 = bf16[128,1536]{1,0:T(8,128)(2,1)} collective-permute-done((bf16[128,1536]{1,0:T(8,128)(2,1)S(1)}, bf16[128,1536]{1,0:T(8,128)(2,1)}, u32[]{:S(2)}, u32[]{:S(2)}) %collective-permute-start.11) | collective-permute-done | bytes 393248 | tf_op jit(solution)/shard_map/ppermute | solution.py:49
  139.7 2.0 collective-permute-start.15
  141.7 3.7 %collective-permute-done.13 = bf16[128,1536]{1,0:T(8,128)(2,1)S(1)} collective-permute-done((bf16[128,1536]{1,0:T(8,128)(2,1)S(1)}, bf16[128,1536]{1,0:T(8,128)(2,1)S(1)}, u32[]{:S(2)}, u32[]{:S(2)}) %collective-permute-start.13) | collective-permute-done | bytes 393248 | tf_op jit(solution)/shard_map/ppermute | solution.py:36
  146.9 6.5 %collective-permute-done.15 = bf16[128,1536]{1,0:T(8,128)(2,1)S(1)} collective-permute-done((bf16[128,1536]{1,0:T(8,128)(2,1)S(1)}, bf16[128,1536]{1,0:T(8,128)(2,1)S(1)}, u32[]{:S(2)}, u32[]{:S(2)}) %collective-permute-start.15) | collective-permute-done | bytes 393248 | tf_op jit(solution)/shard_map/ppermute | solution.py:36
  157.4 3.5 %fusion.6 = f32[512,768]{1,0:T(8,128)S(1)} fusion(bf16[1536,768]{1,0:T(8,128)(2,1)} %all-gather.6.cloned.1.call-done, bf16[1024,1536]{1,0:T(8,128)(2,1)} %constant_dynamic-update-slice_fusion.24, s32[]{:T(128)S(6)} %select_n.159), kind=kOutput, calls=%fused_computation.12 | convolution fusion | flops 1207959552 | bytes 5505028 | tf_op jit(solution)/shard_map/dot_general | solution.py:129
  163.6 21.0 %all-gather.8.cloned.1.call-done = bf16[384,1536]{0,1:T(8,128)(2,1)} async-done(((bf16[384,192]{0,1:T(8,128)(2,1)}), bf16[384,1536]{0,1:T(8,128)(2,1)}) %all-gather.8.cloned.1.call-update) | async-done | bytes 1179664 | tf_op jit(solution)/shard_map/all_gather | solution.py:112
  185.1 8.1 %convolution_convert_fusion.1 = bf16[512,1536]{1,0:T(8,128)(2,1)S(1)} fusion(bf16[384,1536]{0,1:T(8,128)(2,1)} %all-gather.8.cloned.1.call-done, bf16[512,384]{1,0:T(8,128)(2,1)S(1)} %fusion.33, f32[384]{0:T(512)S(1)} %copy-done.29, f32[384]{0:T(512)S(1)} %copy-done.30, f32[384]{0:T(512)S(1)} %get-tuple-element.18, f32[384]{0:T(512)S(1)} %get-tuple-element.19, ...), kind=kOutput, calls=%fused_computation.6 | convolution fusion | flops 629932032 | bytes 3209216 | tf_op jit(solution)/shard_map/dot_general | solution.py:139
  193.2 3.1 %collective-permute-start.16 = (bf16[128,1536]{1,0:T(8,128)(2,1)S(1)}, bf16[128,1536]{1,0:T(8,128)(2,1)S(1)}, u32[]{:S(2)}, u32[]{:S(2)}) collective-permute-start(bf16[128,1536]{1,0:T(8,128)(2,1)S(1)} %get-tuple-element.63), channel_id=1, source_target_pairs={{0,1},{1,2},{2,3},{3,0},{4,5},{5,6},{6,7},{7,4},{8,9},{9,10},{10,1... | collective-permute-start | bytes 1179656 | tf_op jit(solution)/shard_map/ppermute | solution.py:49
  196.8 7.9 %collective-permute-done.16 = bf16[128,1536]{1,0:T(8,128)(2,1)S(1)} collective-permute-done((bf16[128,1536]{1,0:T(8,128)(2,1)S(1)}, bf16[128,1536]{1,0:T(8,128)(2,1)S(1)}, u32[]{:S(2)}, u32[]{:S(2)}) %collective-permute-start.16) | collective-permute-done | bytes 393248 | tf_op jit(solution)/shard_map/ppermute | solution.py:49
  204.6 9.1 %collective-permute-done.17 = bf16[128,1536]{1,0:T(8,128)(2,1)S(1)} collective-permute-done((bf16[128,1536]{1,0:T(8,128)(2,1)S(1)}, bf16[128,1536]{1,0:T(8,128)(2,1)S(1)}, u32[]{:S(2)}, u32[]{:S(2)}) %collective-permute-start.17) | collective-permute-done | bytes 393248 | tf_op jit(solution)/shard_map/ppermute | solution.py:49
  (177 shorter events, 46.4 us)
Async XLA Ops:
  6.5 83.5 %all-gather.4.cloned.1.call-start = ((), (), s32[]{:S(2)}) async-start(), calls=%async_computation | async-start | bytes 3981312 | tf_op jit(solution)/shard_map/all_gather | solution.py:105
  8.5 148.9 %all-gather.6.cloned.1.call-start = ((), (), s32[]{:S(2)}) async-start(), calls=%async_computation.1 | async-start | bytes 2654208 | tf_op jit(solution)/shard_map/all_gather | solution.py:109
  10.3 174.4 %all-gather.8.cloned.1.call-start = ((), (), s32[]{:S(2)}) async-start(), calls=%async_computation.2 | async-start | bytes 1327104 | tf_op jit(solution)/shard_map/all_gather | solution.py:112
  11.7 19.6 %collective-permute-start = (bf16[128,1536]{1,0:T(8,128)(2,1)S(1)}, bf16[128,1536]{1,0:T(8,128)(2,1)S(1)}, u32[]{:S(2)}, u32[]{:S(2)}) collective-permute-start(bf16[128,1536]{1,0:T(8,128)(2,1)S(1)} %get-tuple-element.62), channel_id=1, source_target_pairs={{0,3},{1,0},{2,1},{3,2},{4,7},{5,4},{6,5},{7,6},{8,11},{9,8},{10,9... | collective-permute-start | bytes 1179656 | tf_op jit(solution)/shard_map/ppermute | solution.py:36
  11.8 8.8 %collective-permute-start.3 = (bf16[384,192]{0,1:T(8,128)(2,1)S(1)}, bf16[384,192]{0,1:T(8,128)(2,1)S(1)}, u32[]{:S(2)}, u32[]{:S(2)}) collective-permute-start(bf16[384,192]{0,1:T(8,128)(2,1)S(1)} %copy-done.1), channel_id=1, source_target_pairs={{0,4},{4,8},{8,12},{12,16},{16,20},{20,24},{24,28},{28,0},{1,5},{5... | collective-permute-start | bytes 442376 | tf_op jit(solution)/shard_map/ppermute | solution.py:14
  14.5 17.6 %collective-permute-start.1 = (bf16[128,1536]{1,0:T(8,128)(2,1)S(1)}, bf16[128,1536]{1,0:T(8,128)(2,1)S(1)}, u32[]{:S(2)}, u32[]{:S(2)}) collective-permute-start(bf16[128,1536]{1,0:T(8,128)(2,1)S(1)} %get-tuple-element.62), channel_id=1, source_target_pairs={{0,2},{1,3},{2,0},{3,1},{4,6},{5,7},{6,4},{7,5},{8,10},{9,11},{10,... | collective-permute-start | bytes 1179656 | tf_op jit(solution)/shard_map/ppermute | solution.py:36
  15.7 17.2 %collective-permute-start.2 = (bf16[128,1536]{1,0:T(8,128)(2,1)S(1)}, bf16[128,1536]{1,0:T(8,128)(2,1)S(1)}, u32[]{:S(2)}, u32[]{:S(2)}) collective-permute-start(bf16[128,1536]{1,0:T(8,128)(2,1)S(1)} %get-tuple-element.62), channel_id=1, source_target_pairs={{0,1},{1,2},{2,3},{3,0},{4,5},{5,6},{6,7},{7,4},{8,9},{9,10},{10,1... | collective-permute-start | bytes 1179656 | tf_op jit(solution)/shard_map/ppermute | solution.py:36
  20.6 10.7 %collective-permute-start.4 = (bf16[384,192]{0,1:T(8,128)(2,1)S(1)}, bf16[384,192]{0,1:T(8,128)(2,1)S(1)}, u32[]{:S(2)}, u32[]{:S(2)}) collective-permute-start(bf16[384,192]{0,1:T(8,128)(2,1)S(1)} %collective-permute-done.3), channel_id=1, source_target_pairs={{0,4},{4,8},{8,12},{12,16},{16,20},{20,24},{24,28},{28,0},{1,5},{5... | collective-permute-start | bytes 442376 | tf_op jit(solution)/shard_map/ppermute | solution.py:14
  31.3 10.6 %collective-permute-start.5 = (bf16[384,192]{0,1:T(8,128)(2,1)S(1)}, bf16[384,192]{0,1:T(8,128)(2,1)S(1)}, u32[]{:S(2)}, u32[]{:S(2)}) collective-permute-start(bf16[384,192]{0,1:T(8,128)(2,1)S(1)} %collective-permute-done.4), channel_id=1, source_target_pairs={{0,4},{4,8},{8,12},{12,16},{16,20},{20,24},{24,28},{28,0},{1,5},{5... | collective-permute-start | bytes 442376 | tf_op jit(solution)/shard_map/ppermute | solution.py:14
  41.9 6.7 %collective-permute-start.6 = (bf16[384,192]{0,1:T(8,128)(2,1)S(1)}, bf16[384,192]{0,1:T(8,128)(2,1)S(1)}, u32[]{:S(2)}, u32[]{:S(2)}) collective-permute-start(bf16[384,192]{0,1:T(8,128)(2,1)S(1)} %collective-permute-done.5), channel_id=1, source_target_pairs={{0,4},{4,8},{8,12},{12,16},{16,20},{20,24},{24,28},{28,0},{1,5},{5... | collective-permute-start | bytes 442376 | tf_op jit(solution)/shard_map/ppermute | solution.py:14
  48.6 9.8 %collective-permute-start.7 = (bf16[384,192]{0,1:T(8,128)(2,1)S(1)}, bf16[384,192]{0,1:T(8,128)(2,1)S(1)}, u32[]{:S(2)}, u32[]{:S(2)}) collective-permute-start(bf16[384,192]{0,1:T(8,128)(2,1)S(1)} %collective-permute-done.6), channel_id=1, source_target_pairs={{0,4},{4,8},{8,12},{12,16},{16,20},{20,24},{24,28},{28,0},{1,5},{5... | collective-permute-start | bytes 442376 | tf_op jit(solution)/shard_map/ppermute | solution.py:14
  58.5 9.9 %collective-permute-start.8 = (bf16[384,192]{0,1:T(8,128)(2,1)S(1)}, bf16[384,192]{0,1:T(8,128)(2,1)S(1)}, u32[]{:S(2)}, u32[]{:S(2)}) collective-permute-start(bf16[384,192]{0,1:T(8,128)(2,1)S(1)} %collective-permute-done.7), channel_id=1, source_target_pairs={{0,4},{4,8},{8,12},{12,16},{16,20},{20,24},{24,28},{28,0},{1,5},{5... | collective-permute-start | bytes 442376 | tf_op jit(solution)/shard_map/ppermute | solution.py:14
  68.4 10.3 %collective-permute-start.9 = (bf16[384,192]{0,1:T(8,128)(2,1)S(1)}, bf16[384,192]{0,1:T(8,128)(2,1)S(1)}, u32[]{:S(2)}, u32[]{:S(2)}) collective-permute-start(bf16[384,192]{0,1:T(8,128)(2,1)S(1)} %collective-permute-done.8), channel_id=1, source_target_pairs={{0,4},{4,8},{8,12},{12,16},{16,20},{20,24},{24,28},{28,0},{1,5},{5... | collective-permute-start | bytes 442376 | tf_op jit(solution)/shard_map/ppermute | solution.py:14
  104.1 29.1 %copy-start.3 = (f32[1536]{0:T(1024)S(1)}, f32[1536]{0:T(1024)}, u32[]{:S(2)}) copy-start(f32[1536]{0:T(1024)} %param.12) | copy-start | bytes 18436
  104.2 17.1 %collective-permute-start.10 = (bf16[128,1536]{1,0:T(8,128)(2,1)S(1)}, bf16[128,1536]{1,0:T(8,128)(2,1)}, u32[]{:S(2)}, u32[]{:S(2)}) collective-permute-start(bf16[128,1536]{1,0:T(8,128)(2,1)S(1)} %get-tuple-element.68), channel_id=1, source_target_pairs={{0,1},{1,2},{2,3},{3,0},{4,5},{5,6},{6,7},{7,4},{8,9},{9,10},{10,1... | collective-permute-start | bytes 1179656 | tf_op jit(solution)/shard_map/ppermute | solution.py:49
  113.0 17.7 %collective-permute-start.11 = (bf16[128,1536]{1,0:T(8,128)(2,1)S(1)}, bf16[128,1536]{1,0:T(8,128)(2,1)}, u32[]{:S(2)}, u32[]{:S(2)}) collective-permute-start(bf16[128,1536]{1,0:T(8,128)(2,1)S(1)} %get-tuple-element.70), channel_id=1, source_target_pairs={{0,2},{1,3},{2,0},{3,1},{4,6},{5,7},{6,4},{7,5},{8,10},{9,11},{10,... | collective-permute-start | bytes 1179656 | tf_op jit(solution)/shard_map/ppermute | solution.py:49
  113.2 18.2 %collective-permute-start.12 = (bf16[128,1536]{1,0:T(8,128)(2,1)S(1)}, bf16[128,1536]{1,0:T(8,128)(2,1)}, u32[]{:S(2)}, u32[]{:S(2)}) collective-permute-start(bf16[128,1536]{1,0:T(8,128)(2,1)S(1)} %get-tuple-element.69), channel_id=1, source_target_pairs={{0,3},{1,0},{2,1},{3,2},{4,7},{5,4},{6,5},{7,6},{8,11},{9,8},{10,9... | collective-permute-start | bytes 1179656 | tf_op jit(solution)/shard_map/ppermute | solution.py:49
  134.2 11.2 %collective-permute-start.13 = (bf16[128,1536]{1,0:T(8,128)(2,1)S(1)}, bf16[128,1536]{1,0:T(8,128)(2,1)S(1)}, u32[]{:S(2)}, u32[]{:S(2)}) collective-permute-start(bf16[128,1536]{1,0:T(8,128)(2,1)S(1)} %get-tuple-element.58), channel_id=1, source_target_pairs={{0,3},{1,0},{2,1},{3,2},{4,7},{5,4},{6,5},{7,6},{8,11},{9,8},{10,9... | collective-permute-start | bytes 1179656 | tf_op jit(solution)/shard_map/ppermute | solution.py:36
  134.9 11.3 %collective-permute-start.14 = (bf16[128,1536]{1,0:T(8,128)(2,1)S(1)}, bf16[128,1536]{1,0:T(8,128)(2,1)S(1)}, u32[]{:S(2)}, u32[]{:S(2)}) collective-permute-start(bf16[128,1536]{1,0:T(8,128)(2,1)S(1)} %get-tuple-element.58), channel_id=1, source_target_pairs={{0,2},{1,3},{2,0},{3,1},{4,6},{5,7},{6,4},{7,5},{8,10},{9,11},{10,... | collective-permute-start | bytes 1179656 | tf_op jit(solution)/shard_map/ppermute | solution.py:36
  139.7 13.8 %collective-permute-start.15 = (bf16[128,1536]{1,0:T(8,128)(2,1)S(1)}, bf16[128,1536]{1,0:T(8,128)(2,1)S(1)}, u32[]{:S(2)}, u32[]{:S(2)}) collective-permute-start(bf16[128,1536]{1,0:T(8,128)(2,1)S(1)} %get-tuple-element.58), channel_id=1, source_target_pairs={{0,1},{1,2},{2,3},{3,0},{4,5},{5,6},{6,7},{7,4},{8,9},{9,10},{10,1... | collective-permute-start | bytes 1179656 | tf_op jit(solution)/shard_map/ppermute | solution.py:36
  161.8 22.9 %copy-start.4 = (f32[384]{0:T(512)S(1)}, f32[384]{0:T(512)}, u32[]{:S(2)}) copy-start(f32[384]{0:T(512)} %get-tuple-element.28) | copy-start | bytes 4612
  193.2 11.4 %collective-permute-start.16 = (bf16[128,1536]{1,0:T(8,128)(2,1)S(1)}, bf16[128,1536]{1,0:T(8,128)(2,1)S(1)}, u32[]{:S(2)}, u32[]{:S(2)}) collective-permute-start(bf16[128,1536]{1,0:T(8,128)(2,1)S(1)} %get-tuple-element.63), channel_id=1, source_target_pairs={{0,1},{1,2},{2,3},{3,0},{4,5},{5,6},{6,7},{7,4},{8,9},{9,10},{10,1... | collective-permute-start | bytes 1179656 | tf_op jit(solution)/shard_map/ppermute | solution.py:49
  196.3 17.5 %collective-permute-start.17 = (bf16[128,1536]{1,0:T(8,128)(2,1)S(1)}, bf16[128,1536]{1,0:T(8,128)(2,1)S(1)}, u32[]{:S(2)}, u32[]{:S(2)}) collective-permute-start(bf16[128,1536]{1,0:T(8,128)(2,1)S(1)} %get-tuple-element.65), channel_id=1, source_target_pairs={{0,2},{1,3},{2,0},{3,1},{4,6},{5,7},{6,4},{7,5},{8,10},{9,11},{10,... | collective-permute-start | bytes 1179656 | tf_op jit(solution)/shard_map/ppermute | solution.py:49
  196.6 17.8 %collective-permute-start.18 = (bf16[128,1536]{1,0:T(8,128)(2,1)S(1)}, bf16[128,1536]{1,0:T(8,128)(2,1)S(1)}, u32[]{:S(2)}, u32[]{:S(2)}) collective-permute-start(bf16[128,1536]{1,0:T(8,128)(2,1)S(1)} %get-tuple-element.64), channel_id=1, source_target_pairs={{0,3},{1,0},{2,1},{3,2},{4,7},{5,4},{6,5},{7,6},{8,11},{9,8},{10,9... | collective-permute-start | bytes 1179656 | tf_op jit(solution)/shard_map/ppermute | solution.py:49
  (43 other events, 916.1 us)
Sparse Core Ops, SparseCore 0:
  9.6 80.4 all-gather.3
  92.2 50.6 all-gather.5
  145.1 39.5 all-gather.7
